TPU v7x, 256 devices: a whole 4x4x8 slice. The times are simulated.
256 devices in a mesh: shard: 64 (over y, z, core), cent: 4 (over x).
Axes of the slice: x: 4, y: 4, z: 8, core: 2. Of those that a mesh axis runs over, the one named last changes fastest.
Arguments:
- queries: bfloat16 [1024, 32, 128], P('shard'), may hold values from -6 to 6
- centroids: bfloat16 [196608, 128], P(('shard', 'cent')), may hold values from -0.5 to 0.5
- passages: bfloat16 [16384, 128, 128], P('shard', 'cent'), may hold values from -0.5 to 0.5
- lengths: int32 [16384], P('shard'), may hold values from 16 to 128, as said below
- passage_row: int32 [16384], replicated, may hold values from 0 to 16383, as said below
- candidates: int32 [1024, 16], P('shard'), may hold values from 0 to 16383, as said below
Outputs:
- token_best: float32 [1024, 32], P('shard')
- scores: float32 [1024, 16], P('shard')
Inputs may be any that keep to these rules, and one draw needn't show every extreme that they name: A permutation: passage g is stored at row passage_row[g]. The rows j < lengths[r] of stored passage r are real, the rest padding; the first stored passage of every index of shard has all 128. Among the 256 pairs of the queries of one index of shard, at most 12 have candidates stored at one owner (owner = passage_row[id] // 256); one owner takes exactly 12 pairs from every index of shard.
All inputs are finite; a program needn't handle non-finite values.
Results may differ from a plain program's by a relative error of at most 0.0003.
Values may be sent and summed in bfloat16 or wider, within the bound.
No kernel may reach another device: no remote copies, remote signals or barrier semaphores. Data moves between devices by JAX's collectives and lax.ppermute only.
A program may use at most 128 MiB of HBM per device.

v0:
```python
import jax
import jax.numpy as jnp
from jax import lax
from jax.sharding import PartitionSpec as P

masked_score = -1e30


def per_device(queries, centroids, passages, lengths, passage_row, candidates):
    query_count = queries.shape[0]
    query_tokens = queries.shape[1]
    feature_width = queries.shape[2]
    per_query = candidates.shape[1]
    passage_count = passages.shape[0]
    token_rows = passages.shape[1]
    shard_total = lax.axis_size("shard")
    capacity = max(2, 3 * query_count * per_query // shard_total)
    my_shard = lax.axis_index("shard")
    query_block = lax.all_gather(queries, "shard", axis=0, tiled=True)
    flattened = query_block.reshape(-1, feature_width)
    scored = jnp.einsum("rd,cd->rc", flattened, centroids, preferred_element_type=jnp.float32)
    local_best = jnp.max(scored, axis=1).reshape(query_block.shape[0], query_tokens)
    merged = lax.pmax(local_best, ("shard", "cent"))
    token_best = lax.dynamic_slice_in_dim(merged, my_shard * query_count, query_count, 0)
    pair_rows = jnp.take(passage_row, candidates.reshape(-1), axis=0)
    owners = pair_rows // passage_count
    slot_ids = pair_rows % passage_count
    onehot = (owners[:, None] == jnp.arange(shard_total, dtype=jnp.int32)[None, :]).astype(
        jnp.int32
    )
    ranking = jnp.sum((jnp.cumsum(onehot, axis=0) - onehot) * onehot, axis=1)
    places = owners * capacity + ranking
    pair_query = jnp.arange(query_count * per_query, dtype=jnp.int32) // per_query
    slot_table = (
        jnp.full((shard_total * capacity,), -1, jnp.int32)
        .at[places]
        .set(slot_ids)
        .reshape(shard_total, capacity)
    )
    token_index = lax.axis_index("cent") * token_rows + jnp.arange(token_rows, dtype=jnp.int32)
    flat_queries = queries.reshape(query_count, query_tokens * feature_width)
    token_table = jnp.zeros((shard_total * capacity, query_tokens * feature_width), jnp.bfloat16)
    token_table = token_table.at[places].set(jnp.take(flat_queries, pair_query, axis=0))
    token_table = token_table.reshape(shard_total, capacity, query_tokens * feature_width)
    slot_block = lax.all_to_all(slot_table, "shard", split_axis=0, concat_axis=0, tiled=True)
    safe_slots = jnp.maximum(slot_block, 0).reshape(-1)
    chosen = jnp.take(passages, safe_slots, axis=0)
    asked = lax.all_to_all(token_table, "shard", split_axis=0, concat_axis=0, tiled=True).reshape(
        -1, query_tokens, feature_width
    )
    scored = jnp.einsum("ntd,npd->ntp", asked, chosen, preferred_element_type=jnp.float32)
    valid_tokens = token_index[None, :] < jnp.take(lengths, safe_slots, axis=0)[:, None]
    scored = jnp.where(valid_tokens[:, None, :], scored, masked_score)
    partial_value = jnp.max(scored, axis=2).reshape(
        slot_block.shape[0], slot_block.shape[1], query_tokens
    )
    complete = lax.pmax(partial_value, "cent")
    pair_scores = jnp.sum(complete, axis=2) / query_tokens
    returned = lax.all_to_all(pair_scores, "shard", split_axis=0, concat_axis=0, tiled=True)
    scores = jnp.take(returned.reshape(-1), places, axis=0).reshape(query_count, per_query)
    return (token_best, scores)


def solution(mesh):
    in_specs = (
        P("shard", None, None),
        P(("shard", "cent"), None),
        P("shard", "cent", None),
        P("shard"),
        P(),
        P("shard", None),
    )
    out_specs = (P("shard", None), P("shard", None))
    return jax.shard_map(
        per_device, mesh=mesh, in_specs=in_specs, out_specs=out_specs, check_vma=False
    )
```

profile of v0, /device:TPU:2, one launch (start us, length us, event | category | flops | bytes accessed | tf_op | source)
XLA Modules:
  0.0 633.1 jit_solution(10304121452053333185)
XLA Ops:
  8.0 0.9 reshape.321
  8.9 0.8 reshape.322
  9.7 0.8 reshape.323
  10.5 2.1 gather_fusion
  12.7 0.6 reduce-window.6
  13.6 1.4 scatter_custom_fusion
  15.0 0.7 all_to_all.13
  15.7 12.3 %all-to-all-start = ((s32[64,1,12]{2,1,0:T(1,128)}), s32[64,1,12]{2,1,0:T(1,128)S(1)}, u32[]{:S(2)}, u32[]{:S(2)}) async-start(s32[64,1,12]{2,1,0:T(1,128)} %bitcast.7), calls=%async_computation | async-start | bytes 65536 | tf_op jit(solution)/shard_map/all_to_all | solution.py:45
  28.1 1.0 copy.15
  29.0 13.4 %scatter_custom_fusion.1 = bf16[768,4096]{1,0:T(8,128)(2,1)} fusion(s32[256]{0:T(256)S(1)} %bitcast.44, bf16[]{:T(256)} %constant.143.clone.1, pred[256]{0:T(512)(128)(4,1)S(1)} %compare_and_fusion, bf16[]{:T(256)} %constant.146.clone.1, bf16[16,4096]{1,0:T(8,128)(2,1)S(1)} %bitcast.38, s32[1024]{0:T(1024)S(1)} %pad_clamp_fusion.1), kind=kCustom, calls=%fused_computation.13 | custom fusion | flops 1048576 | bytes 6427140 | tf_op jit(solution)/shard_map/scatter | solution.py:43
  42.5 9.8 %reshape.326 = bf16[64,12,4096]{2,1,0:T(8,128)(2,1)} reshape(bf16[768,4096]{1,0:T(8,128)(2,1)} %scatter_custom_fusion.1) | data formatting | bytes 12582912 | tf_op jit(solution)/shard_map/reshape | solution.py:44
  52.2 10.5 %all-to-all-start.1 = ((bf16[64,12,4096]{2,1,0:T(8,128)(2,1)}), bf16[64,12,4096]{2,1,0:T(8,128)(2,1)}, u32[]{:S(2)}, u32[]{:S(2)}) async-start(bf16[64,12,4096]{2,1,0:T(8,128)(2,1)} %reshape.326), calls=%async_computation.1 | async-start | bytes 16777216 | tf_op jit(solution)/shard_map/all_to_all | solution.py:48
  63.3 5.0 gather_fusion.1
  68.3 4.4 gather_fusion.2
  73.0 174.6 %all-to-all-done.1 = bf16[64,12,4096]{2,1,0:T(8,128)(2,1)} async-done(((bf16[64,12,4096]{2,1,0:T(8,128)(2,1)}), bf16[64,12,4096]{2,1,0:T(8,128)(2,1)}, u32[]{:S(2)}, u32[]{:S(2)}) %all-to-all-start.1) | async-done | bytes 6291488 | tf_op jit(solution)/shard_map/all_to_all | solution.py:48
  247.6 12.2 %reshape.327 = bf16[768,32,128]{2,1,0:T(8,128)(2,1)} reshape(bf16[64,12,4096]{2,1,0:T(8,128)(2,1)} %all-to-all-done.1) | data formatting | bytes 12582912 | tf_op jit(solution)/shard_map/reshape | solution.py:48
  259.8 9.2 %select_reduce_fusion = f32[768,32]{1,0:T(8,128)S(1)} fusion(pred[768,32]{1,0:T(8,128)(4,1)S(1)} %broadcast_compare_fusion, bf16[768,32,128]{2,1,0:T(8,128)(2,1)} %reshape.327, bf16[768,32,128]{2,1,0:T(8,128)(2,1)} %gather_fusion.2, pred[768]{0:T(1024)(128)(4,1)S(1)} %le.92), kind=kOutput, calls=%fused_computation.8 | convolution fusion | flops 206020608 | bytes 12706560 | tf_op jit(solution)/shard_map/ntd,npd->ntp/dot_general | solution.py:51
  268.9 0.9 reshape.328
  269.9 0.5 all-gather.2.cloned.1.call-update
  270.4 44.4 %all-reduce.5.cloned.1.call-done = f32[64,12,32]{2,1,0:T(8,128)} async-done(((f32[64,12,32]{2,1,0:T(8,128)}), f32[64,12,32]{2,1,0:T(8,128)}) %all-reduce.5.cloned.1.call-update) | async-done | bytes 98320 | tf_op jit(solution)/shard_map/pmax | solution.py:57
  314.8 1.3 reduce_sum.25
  316.0 0.6 broadcast_multiply_fusion
  316.6 10.5 %all-to-all-start.2 = ((f32[64,1,12]{2,1,0:T(1,128)}), f32[64,1,12]{2,1,0:T(1,128)S(1)}, u32[]{:S(2)}, u32[]{:S(2)}) async-start(f32[64,1,12]{2,1,0:T(1,128)} %bitcast.9), calls=%async_computation.2 | async-start | bytes 65536 | tf_op jit(solution)/shard_map/all_to_all | solution.py:59
  327.6 9.1 %all-to-all-done.2 = f32[64,1,12]{2,1,0:T(1,128)S(1)} async-done(((f32[64,1,12]{2,1,0:T(1,128)}), f32[64,1,12]{2,1,0:T(1,128)S(1)}, u32[]{:S(2)}, u32[]{:S(2)}) %all-to-all-start.2) | async-done | bytes 3104 | tf_op jit(solution)/shard_map/all_to_all | solution.py:59
  337.2 0.7 reduce.11
  338.0 1.4 gather_fusion.3
  339.5 14.4 %all-gather.2.cloned.1.call-done = bf16[1024,32,128]{2,1,0:T(8,128)(2,1)} async-done(((bf16[16,32,128]{2,1,0:T(8,128)(2,1)}), bf16[1024,32,128]{2,1,0:T(8,128)(2,1)}) %all-gather.2.cloned.1.call-update) | async-done | bytes 8388624 | tf_op jit(solution)/shard_map/all_gather | solution.py:19
  353.9 17.0 %convolution_reduce_fusion = f32[32768]{0:T(1024)S(1)} fusion(bf16[32768,128]{1,0:T(8,128)(2,1)} %bitcast.47, bf16[768,128]{1,0:T(8,128)(2,1)S(1)} %copy-done.3), kind=kOutput, calls=%fused_computation.7 | convolution fusion | flops 6467584000 | bytes 8716288 | tf_op jit(solution)/shard_map/rd,cd->rc/dot_general | solution.py:21
  370.9 1.0 reshape.320
  371.9 0.6 and_select_fusion
  372.6 251.8 %all-reduce.3.cloned.1.call-done = f32[1024,32]{1,0:T(8,128)} async-done(((f32[1024,32]{1,0:T(8,128)}), f32[1024,32]{1,0:T(8,128)}) %all-reduce.3.cloned.1.call-update) | async-done | bytes 131088 | tf_op jit(solution)/shard_map/pmax | solution.py:23
  624.3 1.3 constant_dynamic-slice_fusion
  (42 shorter events, 2.3 us)
Async XLA Ops:
  8.0 60.3 %copy-start = (bf16[256,32,128]{2,1,0:T(8,128)(2,1)S(1)}, bf16[256,32,128]{2,1,0:T(8,128)(2,1)}, u32[]{:S(2)}) copy-start(bf16[256,32,128]{2,1,0:T(8,128)(2,1)} %param.8) | copy-start | bytes 6291460
  15.7 36.5 %all-to-all-start = ((s32[64,1,12]{2,1,0:T(1,128)}), s32[64,1,12]{2,1,0:T(1,128)S(1)}, u32[]{:S(2)}, u32[]{:S(2)}) async-start(s32[64,1,12]{2,1,0:T(1,128)} %bitcast.7), calls=%async_computation | async-start | bytes 65536 | tf_op jit(solution)/shard_map/all_to_all | solution.py:45
  52.2 11.1 %copy-start.1 = (s32[256]{0:T(256)S(1)}, s32[256]{0:T(256)}, u32[]{:S(2)}) copy-start(s32[256]{0:T(256)} %param.9) | copy-start | bytes 3076
  52.2 195.3 %all-to-all-start.1 = ((bf16[64,12,4096]{2,1,0:T(8,128)(2,1)}), bf16[64,12,4096]{2,1,0:T(8,128)(2,1)}, u32[]{:S(2)}, u32[]{:S(2)}) async-start(bf16[64,12,4096]{2,1,0:T(8,128)(2,1)} %reshape.326), calls=%async_computation.1 | async-start | bytes 16777216 | tf_op jit(solution)/shard_map/all_to_all | solution.py:48
  62.8 252.0 %all-reduce.5.cloned.1.call-start = ((), (), s32[]{:S(2)}) async-start(), calls=%async_computation.5 | async-start | bytes 1048576 | tf_op jit(solution)/shard_map/pmax | solution.py:57
  259.7 94.1 %copy-start.3 = (bf16[768,128]{1,0:T(8,128)(2,1)S(1)}, bf16[768,128]{1,0:T(8,128)(2,1)}, u32[]{:S(2)}) copy-start(bf16[768,128]{1,0:T(8,128)(2,1)} %param.7) | copy-start | bytes 589828
  269.8 84.0 %all-gather.2.cloned.1.call-start = ((), (), s32[]{:S(2)}) async-start(), calls=%async_computation.3 | async-start | bytes 8519680 | tf_op jit(solution)/shard_map/all_gather | solution.py:19
  316.6 20.0 %all-to-all-start.2 = ((f32[64,1,12]{2,1,0:T(1,128)}), f32[64,1,12]{2,1,0:T(1,128)S(1)}, u32[]{:S(2)}, u32[]{:S(2)}) async-start(f32[64,1,12]{2,1,0:T(1,128)} %bitcast.9), calls=%async_computation.2 | async-start | bytes 65536 | tf_op jit(solution)/shard_map/all_to_all | solution.py:59
  327.1 297.2 %all-reduce.3.cloned.1.call-start = ((), (), s32[]{:S(2)}) async-start(), calls=%async_computation.4 | async-start | bytes 1048576 | tf_op jit(solution)/shard_map/pmax | solution.py:23
  353.9 18.1 %copy-start.2 = (s32[16,16]{1,0:T(8,128)S(1)}, s32[16,16]{1,0:T(8,128)}, u32[]{:S(2)}) copy-start(s32[16,16]{1,0:T(8,128)} %param.11) | copy-start | bytes 3076
Sparse Core Ops, SparseCore 0:
  270.0 44.7 all-reduce.4
Sparse Core Ops, SparseCore 1:
  273.1 80.7 all-gather.1
  372.0 252.3 all-reduce.2
where the time goes:
time: 634 us; the launch traced here: 633 us
  waiting for transfers between devices  495 us (78%)
  local copies, waits for them, and re-layouts  44.8 us (7%)
  starting transfers between devices  33.7 us (5%)
  matrix products  26.2 us (4%)
  other arithmetic  17.9 us (3%)
  between operations  15.7 us (2%)
    pmax x1, waiting for transfers between devices, per_device(): merged = lax.pmax(local_best, ('shard', 'cent'))  252 us
    all_to_all x1, waiting for transfers between devices, per_device(): lax.all_to_all(token_table, 'shard', split_axis=0, concat_axis=0, tiled=T...  175 us
    pmax x1, waiting for transfers between devices, per_device(): complete = lax.pmax(partial_value, 'cent')  44.4 us
    dot_general x1, matrix products, per_device(): jnp.einsum('rd,cd->rc', flattened, centroids, preferred_element_type=jnp....  17 us
    all_gather x1, waiting for transfers between devices, per_device(): query_block = lax.all_gather(queries, 'shard', axis=0, tiled=True)  14.4 us
    scatter x1, other arithmetic, per_device(): token_table.at[places].set(jnp.take(flat_queries, pair_query, axis=0))  13.4 us
  transfers between devices with their start and end apart: 6, of which 5 were waited for; matrix products, arithmetic and copies ran while one was open for 6% of the time, Pallas kernels for 0%

commit v1 on v0

--- a/solution.py
+++ b/solution.py
@@ -16,7 +16,10 @@
     shard_total = lax.axis_size("shard")
     capacity = max(2, 3 * query_count * per_query // shard_total)
     my_shard = lax.axis_index("shard")
-    query_block = lax.all_gather(queries, "shard", axis=0, tiled=True)
+    query_block = jnp.concatenate(
+        lax.all_to_all(jnp.stack([queries for _ in range(lax.axis_size("shard"))]), "shard", 0, 0),
+        0,
+    )
     flattened = query_block.reshape(-1, feature_width)
     scored = jnp.einsum("rd,cd->rc", flattened, centroids, preferred_element_type=jnp.float32)
     local_best = jnp.max(scored, axis=1).reshape(query_block.shape[0], query_tokens)

time: 634 us -> 813 us (1.28)
  waiting for transfers between devices: 495 us -> 654 us
  blocking collectives: 0 us -> 19.8 us
    all_to_all x1, waiting for transfers between devices: 9.06 us -> 181 us  [per_device(): lax.all_to_all(jnp.stack([queries for _ in range(lax.axis_size('shard'))]...]
    all_to_all x0 -> x1, blocking collectives: none -> 19.8 us  [per_device(): lax.all_to_all(pair_scores, 'shard', split_axis=0, concat_axis=0, tiled=T...]
    all_gather x1 -> x0, waiting for transfers between devices: 14.4 us -> none  [per_device(): query_block = lax.all_gather(queries, 'shard', axis=0, tiled=True)]
  transfers between devices with their start and end apart: 6 -> 5, of which waited for: 5 -> 4; matrix products, arithmetic and copies ran while one was open for 6% -> 5% of each run, Pallas kernels for 0% -> 0%
where the time goes in v1:
time: 813 us; the launch traced here: 812 us
  waiting for transfers between devices  654 us (80%)
  local copies, waits for them, and re-layouts  50 us (6%)
  starting transfers between devices  29.1 us (4%)
  matrix products  26.2 us (3%)
  blocking collectives  19.8 us (2%)
  other arithmetic  17.3 us (2%)
  between operations  15.7 us (2%)
    pmax x1, waiting for transfers between devices, per_device(): merged = lax.pmax(local_best, ('shard', 'cent'))  253 us
    all_to_all x1, waiting for transfers between devices, per_device(): lax.all_to_all(jnp.stack([queries for _ in range(lax.axis_size('shard'))]...  181 us
    all_to_all x1, waiting for transfers between devices, per_device(): lax.all_to_all(token_table, 'shard', split_axis=0, concat_axis=0, tiled=T...  175 us
    pmax x1, waiting for transfers between devices, per_device(): complete = lax.pmax(partial_value, 'cent')  44.9 us
    all_to_all x1, blocking collectives, per_device(): lax.all_to_all(pair_scores, 'shard', split_axis=0, concat_axis=0, tiled=T...  19.8 us
    dot_general x1, matrix products, per_device(): jnp.einsum('rd,cd->rc', flattened, centroids, preferred_element_type=jnp....  17 us
  transfers between devices with their start and end apart: 5, of which 4 were waited for; matrix products, arithmetic and copies ran while one was open for 5% of the time, Pallas kernels for 0%

profile of v1, /device:TPU:2, one launch (start us, length us, event | category | flops | bytes accessed | tf_op | source)
XLA Modules:
  0.0 811.6 jit_solution(5544679996412878956)
XLA Ops:
  8.0 0.9 reshape.319
  8.9 0.8 reshape.320
  9.7 0.8 reshape.321
  10.5 2.1 gather_fusion
  12.7 0.6 reduce-window.6
  13.6 1.4 scatter_custom_fusion
  15.0 0.7 all_to_all.17
  15.7 12.3 %all-to-all-start.1 = ((s32[64,1,12]{2,1,0:T(1,128)}), s32[64,1,12]{2,1,0:T(1,128)S(1)}, u32[]{:S(2)}, u32[]{:S(2)}) async-start(s32[64,1,12]{2,1,0:T(1,128)} %bitcast.7), calls=%async_computation.1 | async-start | bytes 65536 | tf_op jit(solution)/shard_map/all_to_all | solution.py:48
  28.1 1.0 copy.15
  29.0 13.4 %scatter_custom_fusion.1 = bf16[768,4096]{1,0:T(8,128)(2,1)} fusion(s32[256]{0:T(256)S(1)} %bitcast.45, bf16[]{:T(256)} %constant.143.clone.1, pred[256]{0:T(512)(128)(4,1)S(1)} %compare_and_fusion, bf16[]{:T(256)} %constant.146.clone.1, bf16[16,4096]{1,0:T(8,128)(2,1)S(1)} %bitcast.39, s32[1024]{0:T(1024)S(1)} %pad_clamp_fusion.1), kind=kCustom, calls=%fused_computation.13 | custom fusion | flops 1048576 | bytes 6427140 | tf_op jit(solution)/shard_map/scatter | solution.py:46
  42.5 9.8 %reshape.324 = bf16[64,12,4096]{2,1,0:T(8,128)(2,1)} reshape(bf16[768,4096]{1,0:T(8,128)(2,1)} %scatter_custom_fusion.1) | data formatting | bytes 12582912 | tf_op jit(solution)/shard_map/reshape | solution.py:47
  52.2 10.5 %all-to-all-start.2 = ((bf16[64,12,4096]{2,1,0:T(8,128)(2,1)}), bf16[64,12,4096]{2,1,0:T(8,128)(2,1)}, u32[]{:S(2)}, u32[]{:S(2)}) async-start(bf16[64,12,4096]{2,1,0:T(8,128)(2,1)} %reshape.324), calls=%async_computation.2 | async-start | bytes 16777216 | tf_op jit(solution)/shard_map/all_to_all | solution.py:51
  63.3 5.0 gather_fusion.1
  68.3 4.4 gather_fusion.2
  73.0 174.6 %all-to-all-done.2 = bf16[64,12,4096]{2,1,0:T(8,128)(2,1)} async-done(((bf16[64,12,4096]{2,1,0:T(8,128)(2,1)}), bf16[64,12,4096]{2,1,0:T(8,128)(2,1)}, u32[]{:S(2)}, u32[]{:S(2)}) %all-to-all-start.2) | async-done | bytes 6291488 | tf_op jit(solution)/shard_map/all_to_all | solution.py:51
  247.6 12.2 %reshape.325 = bf16[768,32,128]{2,1,0:T(8,128)(2,1)} reshape(bf16[64,12,4096]{2,1,0:T(8,128)(2,1)} %all-to-all-done.2) | data formatting | bytes 12582912 | tf_op jit(solution)/shard_map/reshape | solution.py:51
  259.8 9.1 %select_reduce_fusion = f32[768,32]{1,0:T(8,128)S(1)} fusion(pred[768,32]{1,0:T(8,128)(4,1)S(1)} %broadcast_compare_fusion, bf16[768,32,128]{2,1,0:T(8,128)(2,1)} %reshape.325, bf16[768,32,128]{2,1,0:T(8,128)(2,1)} %gather_fusion.2, pred[768]{0:T(1024)(128)(4,1)S(1)} %le.92), kind=kOutput, calls=%fused_computation.8 | convolution fusion | flops 206020608 | bytes 12706560 | tf_op jit(solution)/shard_map/ntd,npd->ntp/dot_general | solution.py:54
  268.9 0.8 reshape.326
  269.8 44.9 %all-reduce.5.cloned.1.call-done = f32[64,12,32]{2,1,0:T(8,128)} async-done(((f32[64,12,32]{2,1,0:T(8,128)}), f32[64,12,32]{2,1,0:T(8,128)}) %all-reduce.5.cloned.1.call-update) | async-done | bytes 98320 | tf_op jit(solution)/shard_map/pmax | solution.py:60
  314.7 1.3 reduce_sum.25
  315.9 19.8 %all_to_all.25 = f32[64,1,12]{2,1,0:T(1,128)S(1)} all-to-all(f32[64,1,12]{2,1,0:T(1,128)S(1)} %bitcast.40), channel_id=1, replica_groups=mesh['shard'=64,'cent'=4] {'shard'}, dimensions={0} | all-to-all | bytes 6144 | tf_op jit(solution)/shard_map/all_to_all | solution.py:62
  335.7 5.2 stack.2
  341.0 5.9 all-to-all-start
  347.3 0.5 broadcast.434
  347.9 0.7 reduce.11
  348.7 1.4 gather_fusion.3
  350.1 181.5 %all-to-all-done = bf16[64,16,32,128]{3,2,1,0:T(8,128)(2,1)} async-done(((bf16[64,16,32,128]{3,2,1,0:T(8,128)(2,1)}), bf16[64,16,32,128]{3,2,1,0:T(8,128)(2,1)}, u32[]{:S(2)}, u32[]{:S(2)}) %all-to-all-start) | async-done | bytes 8388640 | tf_op jit(solution)/shard_map/all_to_all | solution.py:20
  531.6 17.0 %convolution_reduce_fusion = f32[32768]{0:T(1024)S(1)} fusion(bf16[32768,128]{1,0:T(8,128)(2,1)} %bitcast, bf16[768,128]{1,0:T(8,128)(2,1)S(1)} %copy-done.4), kind=kOutput, calls=%fused_computation.7 | convolution fusion | flops 6467584000 | bytes 8716288 | tf_op jit(solution)/shard_map/rd,cd->rc/dot_general | solution.py:24
  548.7 1.0 reshape.318
  549.7 0.6 and_select_fusion
  550.3 252.5 %all-reduce.3.cloned.1.call-done = f32[1024,32]{1,0:T(8,128)} async-done(((f32[1024,32]{1,0:T(8,128)}), f32[1024,32]{1,0:T(8,128)}) %all-reduce.3.cloned.1.call-update) | async-done | bytes 131088 | tf_op jit(solution)/shard_map/pmax | solution.py:26
  802.9 1.3 constant_dynamic-slice_fusion
  (43 shorter events, 1.8 us)
Async XLA Ops:
  8.0 60.3 %copy-start = (bf16[256,32,128]{2,1,0:T(8,128)(2,1)S(1)}, bf16[256,32,128]{2,1,0:T(8,128)(2,1)}, u32[]{:S(2)}) copy-start(bf16[256,32,128]{2,1,0:T(8,128)(2,1)} %param.8) | copy-start | bytes 6291460
  15.7 36.5 %all-to-all-start.1 = ((s32[64,1,12]{2,1,0:T(1,128)}), s32[64,1,12]{2,1,0:T(1,128)S(1)}, u32[]{:S(2)}, u32[]{:S(2)}) async-start(s32[64,1,12]{2,1,0:T(1,128)} %bitcast.7), calls=%async_computation.1 | async-start | bytes 65536 | tf_op jit(solution)/shard_map/all_to_all | solution.py:48
  52.2 11.1 %copy-start.1 = (s32[256]{0:T(256)S(1)}, s32[256]{0:T(256)}, u32[]{:S(2)}) copy-start(s32[256]{0:T(256)} %param.9) | copy-start | bytes 3076
  52.2 195.3 %all-to-all-start.2 = ((bf16[64,12,4096]{2,1,0:T(8,128)(2,1)}), bf16[64,12,4096]{2,1,0:T(8,128)(2,1)}, u32[]{:S(2)}, u32[]{:S(2)}) async-start(bf16[64,12,4096]{2,1,0:T(8,128)(2,1)} %reshape.324), calls=%async_computation.2 | async-start | bytes 16777216 | tf_op jit(solution)/shard_map/all_to_all | solution.py:51
  62.8 251.9 %all-reduce.5.cloned.1.call-start = ((), (), s32[]{:S(2)}) async-start(), calls=%async_computation.5 | async-start | bytes 1048576 | tf_op jit(solution)/shard_map/pmax | solution.py:60
  259.7 76.0 %copy-start.2 = (bf16[16,32,128]{2,1,0:T(8,128)(2,1)S(1)}, bf16[16,32,128]{2,1,0:T(8,128)(2,1)}, u32[]{:S(2)}) copy-start(bf16[16,32,128]{2,1,0:T(8,128)(2,1)} %param.6) | copy-start | bytes 393220
  341.0 190.7 %copy-start.4 = (bf16[768,128]{1,0:T(8,128)(2,1)S(1)}, bf16[768,128]{1,0:T(8,128)(2,1)}, u32[]{:S(2)}) copy-start(bf16[768,128]{1,0:T(8,128)(2,1)} %param.7) | copy-start | bytes 589828
  341.0 190.7 %all-to-all-start = ((bf16[64,16,32,128]{3,2,1,0:T(8,128)(2,1)}), bf16[64,16,32,128]{3,2,1,0:T(8,128)(2,1)}, u32[]{:S(2)}, u32[]{:S(2)}) async-start(bf16[64,16,32,128]{3,2,1,0:T(8,128)(2,1)} %stack.2), calls=%async_computation | async-start | bytes 16777216 | tf_op jit(solution)/shard_map/all_to_all | solution.py:20
  346.9 456.0 %all-reduce.3.cloned.1.call-start = ((), (), s32[]{:S(2)}) async-start(), calls=%async_computation.4 | async-start | bytes 1048576 | tf_op jit(solution)/shard_map/pmax | solution.py:26
  531.6 18.1 %copy-start.3 = (s32[16,16]{1,0:T(8,128)S(1)}, s32[16,16]{1,0:T(8,128)}, u32[]{:S(2)}) copy-start(s32[16,16]{1,0:T(8,128)} %param.11) | copy-start | bytes 3076
Sparse Core Ops, SparseCore 0:
  269.9 44.7 all-reduce.4
Sparse Core Ops, SparseCore 1:
  549.8 253.0 all-reduce.2
